TPU v7x, 256 devices: a whole 4x4x8 slice. The times are simulated.
256 devices in a mesh: view: 16 (over z, y_hi), row: 16 (over x, y_lo, core).
Axes of the slice: x: 4, y: 4 (y_hi: 2, y_lo: 2; y = y_hi * 2 + y_lo), z: 8, core: 2. Of those that a mesh axis runs over, the one named last changes fastest.
Arguments:
- latent: bfloat16 [1, 16, 32, 72, 1280], P(None, 'view', 'row'), may hold values from -30 to 30
- gn_gain: float32 [1280], replicated, may hold values from 0.25 to 1.75
- gn_bias: float32 [1280], replicated, may hold values from -3 to 3
- cam_idx: int32 [1, 16], P(None, 'view'), may hold values from 0 to 63
- noise_idx: int32 [1], replicated, may hold values from 0 to 999
- cam_table: bfloat16 [64, 2560], replicated, may hold values from -2 to 2
- noise_table: bfloat16 [1000, 2560], replicated, may hold values from -2 to 2
- conv_w: bfloat16 [3, 3, 1280, 1280], P(None, None, None, 'row'), may hold values from -0.0546875 to 0.0546875
- conv_bias: float32 [1280], replicated, may hold values from -3 to 3
- ln_gain: float32 [1280], replicated, may hold values from 0.25 to 1.75
- attn_in: bfloat16 [3, 1280, 1280], P(None, None, 'view'), may hold values from -0.15625 to 0.15625
- attn_out: bfloat16 [1280, 1280], P('view'), may hold values from -0.15625 to 0.15625
- head_scale: float32 [20], replicated, may hold values from 0.4 to 135
Outputs:
- block_out: bfloat16 [1, 16, 32, 72, 1280], P(None, 'view', 'row')
All inputs are finite; a program needn't handle non-finite values.
Results may differ from a plain program's by a relative error of at most 0.02.
Values may be sent and summed in bfloat16 or wider, within the bound.
No kernel may reach another device: no remote copies, remote signals or barrier semaphores. Data moves between devices by JAX's collectives and lax.ppermute only.
A program may use at most 192 MiB of HBM per device.

v0:
```python
import math
import jax
import jax.numpy as jnp
from jax import lax
from jax.sharding import PartitionSpec as P

GROUPS = 32
epsilon = 1e-05


def attend(query, key_block, value, head_scale):
    view_count = query.shape[0]
    item_count = query.shape[2]
    channels = query.shape[3]
    head_count = head_scale.shape[0]
    head_size = channels // head_count
    query_heads = query.reshape(view_count, item_count, head_count, head_size)
    key_heads = key_block.reshape(view_count, item_count, head_count, head_size)
    value_heads = value.reshape(view_count, item_count, head_count, head_size)
    scores = jnp.einsum(
        "vihd,uihd->ihvu", query_heads, key_heads, preferred_element_type=jnp.float32
    )
    scores = scores * (head_scale / math.sqrt(head_size))[None, :, None, None]
    peak_score = jnp.max(scores, axis=-1, keepdims=True)
    exp_scores = jnp.exp(scores - peak_score)
    soft_weights = (exp_scores / jnp.sum(exp_scores, axis=-1, keepdims=True)).astype(jnp.bfloat16)
    mixed = jnp.einsum(
        "ihvu,uihd->vihd", soft_weights, value_heads, preferred_element_type=jnp.float32
    )
    return mixed.astype(jnp.bfloat16).reshape(view_count, 1, item_count, channels)


def send_back(mixed):
    return lax.all_to_all(mixed, "view", split_axis=0, concat_axis=1, tiled=True)


def local(
    latent,
    gn_gain,
    gn_bias,
    cam_idx,
    noise_idx,
    cam_table,
    noise_table,
    conv_w,
    conv_bias,
    ln_gain,
    attn_in,
    attn_out,
    head_scale,
):
    samples, local_views, local_rows, local_cols, channels = latent.shape
    width_out = ln_gain.shape[0]
    out_part = conv_w.shape[-1]
    whole = lax.all_gather(latent, ROW, axis=2, tiled=True)
    whole, attn_in, attn_out = lax.optimization_barrier((whole, attn_in, attn_out))
    core = lax.axis_index("core")
    half_in = attn_in.shape[1] // 2
    half_out = attn_out.shape[1] // 2
    in_half = lax.dynamic_slice_in_dim(attn_in, core * half_in, half_in, axis=1)
    in_half = lax.all_gather(in_half, "view", axis=0, tiled=False)
    out_half = lax.dynamic_slice_in_dim(attn_out, core * half_out, half_out, axis=1)
    all_rows = whole.shape[2]
    x_float = whole.astype(jnp.float32)
    grouped = x_float.reshape(
        samples, local_views, all_rows, local_cols, GROUPS, channels // GROUPS
    )
    average = jnp.mean(grouped, axis=(2, 3, 5), keepdims=True)
    centred = grouped - average
    variance = jnp.mean(centred * centred, axis=(2, 3, 5), keepdims=True)
    normed = (centred * lax.rsqrt(variance + epsilon)).reshape(x_float.shape)
    cam_hot = (cam_idx[:, :, None] == jnp.arange(cam_table.shape[0], dtype=jnp.int32)).astype(
        jnp.bfloat16
    )
    cam_film = jnp.einsum("svn,nc->svc", cam_hot, cam_table, preferred_element_type=jnp.float32)
    noise_hot = (noise_idx[:, None] == jnp.arange(noise_table.shape[0], dtype=jnp.int32)).astype(
        jnp.bfloat16
    )
    noise_film = jnp.dot(noise_hot, noise_table, preferred_element_type=jnp.float32)
    film_rows = cam_film + noise_film[:, None, :]
    film_scale = film_rows[:, :, None, None, :channels]
    film_shift = film_rows[:, :, None, None, channels:]
    hidden = (normed * gn_gain + gn_bias) * (1.0 + film_scale) + film_shift
    activated = jax.nn.silu(hidden).astype(jnp.bfloat16)
    conv_out = lax.conv_general_dilated(
        activated.reshape(samples * local_views, all_rows, local_cols, channels),
        conv_w,
        window_strides=(1, 1),
        padding=((1, 1), (1, 1)),
        dimension_numbers=("NHWC", "HWIO", "NHWC"),
        preferred_element_type=jnp.float32,
    ).reshape(samples, local_views, all_rows, local_cols, out_part)
    me = lax.axis_index("chip") * lax.axis_size("core") + core
    bias_part = lax.dynamic_slice_in_dim(conv_bias, me * out_part, out_part)
    latent_part = lax.dynamic_slice_in_dim(whole, me * out_part, out_part, axis=4)
    resid_part = (latent_part.astype(jnp.float32) + conv_out + bias_part).astype(jnp.bfloat16)
    in_half, resid_part = lax.optimization_barrier((in_half, resid_part))
    weights_in = lax.all_gather(in_half, "core", axis=0, tiled=False)
    resid_out = lax.all_to_all(resid_part, ROW, split_axis=2, concat_axis=4, tiled=True)
    resid_float = resid_out.astype(jnp.float32)
    middle = jnp.mean(resid_float, axis=-1, keepdims=True)
    spread_y = jnp.mean((resid_float - middle) ** 2, axis=-1, keepdims=True)
    normed_y = ((resid_float - middle) * lax.rsqrt(spread_y + epsilon) * ln_gain).astype(
        jnp.bfloat16
    )
    view_devices = lax.axis_size("view")
    per_device = samples * local_rows * local_cols // view_devices
    pixel_major = jnp.moveaxis(normed_y, 1, 0).reshape(
        local_views, view_devices, per_device, width_out
    )
    flat_block = pixel_major.reshape(-1, 2, width_out // 2)
    triple_in = jnp.einsum(
        "pkc,kjmcd->mpjd", flat_block, weights_in, preferred_element_type=jnp.float32
    ).astype(jnp.bfloat16)
    triple_in = triple_in.reshape((3,) + pixel_major.shape)
    out_half, triple_in = lax.optimization_barrier((out_half, triple_in))
    out_half = lax.all_gather(out_half, "view", axis=0, tiled=True)
    triple_in = lax.all_to_all(triple_in, "view", split_axis=2, concat_axis=1, tiled=True)
    mixed = send_back(attend(triple_in[0], triple_in[1], triple_in[2], head_scale))
    out_half, mixed = lax.optimization_barrier((out_half, mixed))
    weights_out = lax.all_gather(out_half, "core", axis=0, tiled=False)
    mixed = jnp.moveaxis(
        mixed.reshape(local_views, samples, local_rows, local_cols, width_out), 0, 1
    )
    flat_mixed = mixed.reshape(-1, width_out)
    projected = jnp.einsum(
        "pc,kcd->pkd", flat_mixed, weights_out, preferred_element_type=jnp.float32
    )
    return (resid_float + projected.reshape(resid_float.shape)).astype(jnp.bfloat16)


ROW = ("chip", "core")


def solution(mesh):
    cores = 2
    split = jax.sharding.Mesh(
        mesh.devices.reshape(mesh.shape["view"], mesh.shape["row"] // cores, cores),
        ("view", "chip", "core"),
    )
    placed = (
        P(None, "view", ROW, None, None),
        P(),
        P(),
        P(None, "view"),
        P(),
        P(),
        P(),
        P(None, None, None, ROW),
        P(),
        P(),
        P(None, None, "view"),
        P("view", None),
        P(),
    )
    return jax.shard_map(
        local,
        mesh=split,
        in_specs=placed,
        out_specs=P(None, "view", ROW, None, None),
        check_vma=False,
    )
```

profile of v0, /device:TPU:1, one launch (start us, length us, event | category | flops | bytes accessed | tf_op | source)
XLA Modules:
  0.0 350.6 jit_solution(10321813126953900763)
XLA Ops:
  7.3 49.7 %all-gather.9.cloned.1.call-done = bf16[1,1,32,72,1280]{4,3,1,0,2:T(8,128)(2,1)} async-done(((bf16[1,1,2,72,1280]{4,3,1,0,2:T(8,128)(2,1)}), bf16[1,1,32,72,1280]{4,3,1,0,2:T(8,128)(2,1)}) %all-gather.9.cloned.1.call-update) | async-done | bytes 5898256 | tf_op jit(solution)/shard_map/all_gather | solution.py:55
  61.2 3.4 convolution_reduce_fusion
  67.9 6.8 %copy.79 = bf16[1,1,32,72,1280]{4,2,3,1,0:T(8,128)(2,1)} copy(bf16[1,1,32,72,1280]{4,3,1,0,2:T(8,128)(2,1)} %all-gather.9.cloned.1.call-done) | data formatting | bytes 11796480 | tf_op jit(solution)/shard_map/optimization_barrier | solution.py:56
  75.9 4.5 %fusion.4 = f32[1280]{0:T(1024)S(1)} fusion(f32[1280]{0:T(1024)S(1)} %sub.48, bf16[1,1,32,72,1280]{4,3,1,0,2:T(8,128)(2,1)} %all-gather.9.cloned.1.call-done), kind=kLoop, calls=%fused_computation.7 | loop fusion | flops 11795200 | bytes 5908480 | tf_op jit(solution)/shard_map/reduce_sum | solution.py:70
  80.8 8.7 %fusion.16 = bf16[32,1,72,1280]{3,0,2,1:T(8,128)(2,1)S(1)} fusion(f32[1280]{0:T(1024)S(1)} %copy-done.4, f32[1280]{0:T(1024)S(1)} %copy-done.3, f32[1280]{0:T(1024)S(1)} %copy-done.6, f32[1280]{0:T(1024)S(1)} %copy-done.7, f32[1280]{0:T(1024)S(1)} %mul.96, f32[1280]{0:T(1024)S(1)} %sub.48, bf16[1,1,32,72,1280]{4,3,1,0,2:T(8,128)(2,1)} %all-gather.9.cloned.1.call-done), kind=kLoop, calls=%fused_computation.19 | loop fusion | flops 35389440 | bytes 11827200 | tf_op jit(solution)/shard_map/reshape | solution.py:86
  90.3 3.6 %copy.82 = bf16[32,1,8,10,1280]{4,2,3,0,1:T(8,128)(2,1)S(1)} copy(bf16[32,1,8,10,1280]{4,0,3,2,1:T(8,128)(2,1)S(1)} %bitcast.78) | data formatting | bytes 13107200 | tf_op jit(solution)/shard_map/conv_general_dilated | solution.py:85
  94.3 17.0 %fusion.23 = f32[32,8,10,80]{3,1,2,0:T(8,128)S(1)} fusion(bf16[3,3,1280,80]{2,3,1,0:T(8,128)(2,1)S(1)} %copy-done, bf16[32,1,7,2,1280]{4,2,3,0,1:T(8,128)(2,1)S(1)} %slice.28, bf16[32,1,8,10,1280]{4,2,3,0,1:T(8,128)(2,1)S(1)} %copy.82, pred[8,10]{0,1:T(8,128)(4,1)S(1)} %copy-done.10), kind=kOutput, calls=%fused_computation.31 | convolution fusion | flops 4644085760 | bytes 10362960 | tf_op jit(solution)/shard_map/conv_general_dilated | solution.py:85
  113.4 48.8 %all-gather.13.cloned.1.call-done = bf16[48,640,80]{1,2,0:T(8,128)(2,1)} async-done(((bf16[3,640,80]{1,2,0:T(8,128)(2,1)}), bf16[48,640,80]{1,2,0:T(8,128)(2,1)}) %all-gather.13.cloned.1.call-update) | async-done | bytes 4915216 | tf_op jit(solution)/shard_map/all_gather | solution.py:61
  163.2 7.9 %all-to-all-start = ((bf16[1,1,32,72,80]{4,3,1,0,2:T(8,128)(2,1)}), bf16[1,1,32,72,80]{4,3,1,0,2:T(8,128)(2,1)S(1)}, u32[]{:S(2)}, u32[]{:S(2)}) async-start(bf16[1,1,32,72,80]{4,3,1,0,2:T(8,128)(2,1)} %copy.84), calls=%async_computation | async-start | bytes 1179648 | tf_op jit(solution)/shard_map/all_to_all | solution.py:99
  171.8 9.4 %all-to-all-done = bf16[1,1,32,72,80]{4,3,1,0,2:T(8,128)(2,1)S(1)} async-done(((bf16[1,1,32,72,80]{4,3,1,0,2:T(8,128)(2,1)}), bf16[1,1,32,72,80]{4,3,1,0,2:T(8,128)(2,1)S(1)}, u32[]{:S(2)}, u32[]{:S(2)}) %all-to-all-start) | async-done | bytes 368672 | tf_op jit(solution)/shard_map/all_to_all | solution.py:99
  185.3 6.5 %all-gather.15.cloned.1.call-done = bf16[32,3,640,80]{2,3,1,0:T(8,128)(2,1)} async-done(((bf16[16,3,640,80]{2,3,1,0:T(8,128)(2,1)}), bf16[32,3,640,80]{2,3,1,0:T(8,128)(2,1)}) %all-gather.15.cloned.1.call-update) | async-done | bytes 9830416 | tf_op jit(solution)/shard_map/all_gather | solution.py:98
  191.8 8.2 %fusion.38 = bf16[16,3,80,144,1]{2,3,1,0,4:T(8,128)(2,1)S(1)} fusion(bf16[2,16,3,640,80]{3,4,2,1,0:T(8,128)(2,1)} %bitcast.91, f32[144,2,640]{2,1,0:T(2,128)S(1)} %reshape.199, f32[2,640]{1,0:T(2,128)S(1)} %mul.106, f32[144]{0:T(256)S(1)} %rsqrt.21, f32[144]{0:T(256)S(1)} %div.35), kind=kOutput, calls=%fused_computation.53 | convolution fusion | flops 1416314880 | bytes 11679872 | tf_op jit(solution)/shard_map/pkc,kjmcd->mpjd/dot_general | solution.py:112
  201.8 5.7 %reshape.189 = bf16[3,1,16,9,1280]{4,0,3,2,1:T(4,128)(2,1)} reshape(bf16[3,144,16,80]{3,2,0,1:T(8,128)(2,1)} %copy.88) | data formatting | bytes 2211840 | tf_op jit(solution)/shard_map/reshape | solution.py:115
  207.5 9.0 %all-to-all-start.1 = ((bf16[3,1,16,9,1280]{4,0,3,1,2:T(4,128)(2,1)}), bf16[3,1,16,9,1280]{4,0,3,1,2:T(4,128)(2,1)S(1)}, u32[]{:S(2)}, u32[]{:S(2)}) async-start(bf16[3,1,16,9,1280]{4,0,3,1,2:T(4,128)(2,1)} %bitcast.83), calls=%async_computation.1 | async-start | bytes 2949120 | tf_op jit(solution)/shard_map/all_to_all | solution.py:118
  217.1 36.4 %all-to-all-done.1 = bf16[3,1,16,9,1280]{4,0,3,1,2:T(4,128)(2,1)S(1)} async-done(((bf16[3,1,16,9,1280]{4,0,3,1,2:T(4,128)(2,1)}), bf16[3,1,16,9,1280]{4,0,3,1,2:T(4,128)(2,1)S(1)}, u32[]{:S(2)}, u32[]{:S(2)}) %all-to-all-start.1) | async-done | bytes 1105952 | tf_op jit(solution)/shard_map/all_to_all | solution.py:118
  253.5 6.4 %slice_reduce_fusion.2 = (bf16[16,9,1280]{2,1,0:T(8,128)(2,1)S(1)}, bf16[16,9,1280]{2,1,0:T(8,128)(2,1)}, bf16[16,9,1280]{2,1,0:T(8,128)(2,1)}) fusion(bf16[3,1,16,9,1280]{4,0,3,1,2:T(4,128)(2,1)S(1)} %all-to-all-done.1), kind=kLoop, calls=%fused_computation.43 | loop fusion | bytes 2211840 | tf_op jit(solution)/shard_map/slice | solution.py:119
  261.7 2.5 reshape.222
  265.7 3.2 fusion.56
  268.9 2.1 fusion.26
  271.8 29.6 %all_to_all.30 = bf16[16,1,9,1280]{3,2,1,0:T(8,128)(2,1)S(1)} all-to-all(bf16[16,1,9,1280]{3,2,1,0:T(8,128)(2,1)S(1)} %reshape.223), channel_id=1, replica_groups=mesh['view'=16,'chip'=8,'core'=2] {'view'}, dimensions={0} | all-to-all | bytes 737280 | tf_op jit(solution)/shard_map/all_to_all | solution.py:34
  301.4 10.8 %all-gather.11.cloned.1.call-done = bf16[1280,640]{1,0:T(8,128)(2,1)} async-done(((bf16[80,640]{1,0:T(8,128)(2,1)}), bf16[1280,640]{1,0:T(8,128)(2,1)}) %all-gather.11.cloned.1.call-update) | async-done | bytes 1638416 | tf_op jit(solution)/shard_map/all_gather | solution.py:117
  313.0 21.1 %all-gather.17.cloned.1.call-done = bf16[2560,640]{1,0:T(8,128)(2,1)} async-done(((bf16[1280,640]{1,0:T(8,128)(2,1)}), bf16[2560,640]{1,0:T(8,128)(2,1)}) %all-gather.17.cloned.1.call-update) | async-done | bytes 3276816 | tf_op jit(solution)/shard_map/all_gather | solution.py:121
  334.2 5.7 %copy.99 = bf16[2,1280,640]{1,2,0:T(8,128)(2,1)} copy(bf16[2,1280,640]{2,1,0:T(8,128)(2,1)} %bitcast.88) | data formatting | bytes 6553600 | tf_op jit(solution)/shard_map/all_gather | solution.py:121
  339.9 3.9 %fusion.19 = bf16[1,1,2,72,1280]{4,3,2,1,0:T(8,128)(2,1)} fusion(f32[2,72,1280]{2,1,0:T(8,128)S(1)} %reshape.198, bf16[2,72,1280]{2,1,0:T(8,128)(2,1)S(1)} %dot_general.29, bf16[1280,1280,1]{1,0,2:T(8,128)(2,1)} %bitcast.79), kind=kOutput, calls=%fused_computation.24 | convolution fusion | flops 472227840 | bytes 4751360 | tf_op jit(solution)/shard_map/pc,kcd->pkd/dot_general | solution.py:126
  (81 shorter events, 24.8 us)
Async XLA Ops:
  6.5 87.7 %copy-start = (bf16[3,3,1280,80]{2,3,1,0:T(8,128)(2,1)S(1)}, bf16[3,3,1280,80]{2,3,1,0:T(8,128)(2,1)}, u32[]{:S(2)}) copy-start(bf16[3,3,1280,80]{2,3,1,0:T(8,128)(2,1)} %param.20) | copy-start | bytes 5529604
  6.5 50.4 %all-gather.9.cloned.1.call-start = ((), (), s32[]{:S(2)}) async-start(), calls=%async_computation.3 | async-start | bytes 6266880 | tf_op jit(solution)/shard_map/all_gather | solution.py:55
  7.3 154.9 %all-gather.13.cloned.1.call-start = ((), (), s32[]{:S(2)}) async-start(), calls=%async_computation.5 | async-start | bytes 5222400 | tf_op jit(solution)/shard_map/all_gather | solution.py:61
  58.7 133.1 %all-gather.15.cloned.1.call-start = ((), (), s32[]{:S(2)}) async-start(), calls=%async_computation.6 | async-start | bytes 14745600 | tf_op jit(solution)/shard_map/all_gather | solution.py:98
  61.2 13.4 %slice-start = ((s8[5898240]{0:T(1024)(128)(4,1)}), s8[1703936]{0:T(1024)(128)(4,1)S(1)}, s32[]{:S(2)}) async-start(s8[5898240]{0:T(1024)(128)(4,1)} %bitcast.76), calls=%async_computation.8 | async-start | bytes 3407872
  67.9 6.8 %slice-start.1 = ((s8[5898240]{0:T(1024)(128)(4,1)}), s8[4194304]{0:T(1024)(128)(4,1)S(1)}, s32[]{:S(2)}) async-start(s8[5898240]{0:T(1024)(128)(4,1)} %bitcast.76), calls=%async_computation.9 | async-start | bytes 8388608
  75.5 5.3 %copy-start.3 = (f32[1280]{0:T(1024)S(1)}, f32[1280]{0:T(1024)}, u32[]{:S(2)}) copy-start(f32[1280]{0:T(1024)} %get-tuple-element.26) | copy-start | bytes 15364
  75.5 5.3 %copy-start.4 = (f32[1280]{0:T(1024)S(1)}, f32[1280]{0:T(1024)}, u32[]{:S(2)}) copy-start(f32[1280]{0:T(1024)} %get-tuple-element.27) | copy-start | bytes 15364
  75.5 5.3 %copy-start.6 = (f32[1280]{0:T(1024)S(1)}, f32[1280]{0:T(1024)}, u32[]{:S(2)}) copy-start(f32[1280]{0:T(1024)} %param.15) | copy-start | bytes 15364
  75.5 5.3 %copy-start.7 = (f32[1280]{0:T(1024)S(1)}, f32[1280]{0:T(1024)}, u32[]{:S(2)}) copy-start(f32[1280]{0:T(1024)} %param.14) | copy-start | bytes 15364
  90.3 4.0 %copy-start.10 = (pred[8,10]{0,1:T(8,128)(4,1)S(1)}, pred[8,10]{0,1:T(8,128)(4,1)}, u32[]{:S(2)}) copy-start(pred[8,10]{0,1:T(8,128)(4,1)} %constant.46) | copy-start | bytes 244
  94.3 17.4 %copy-start.8 = (f32[80]{0:T(128)S(1)}, f32[80]{0:T(128)}, u32[]{:S(2)}) copy-start(f32[80]{0:T(128)} %dynamic_slice.14) | copy-start | bytes 964
  111.7 59.4 %copy-start.5 = (f32[1280]{0:T(1024)S(1)}, f32[1280]{0:T(1024)}, u32[]{:S(2)}) copy-start(f32[1280]{0:T(1024)} %param.22) | copy-start | bytes 15364
  111.7 59.5 %copy-start.2 = (bf16[80,1280]{1,0:T(8,128)(2,1)S(1)}, bf16[80,1280]{1,0:T(8,128)(2,1)}, u32[]{:S(2)}) copy-start(bf16[80,1280]{1,0:T(8,128)(2,1)} %param.24) | copy-start | bytes 614404
  163.2 17.9 %all-to-all-start = ((bf16[1,1,32,72,80]{4,3,1,0,2:T(8,128)(2,1)}), bf16[1,1,32,72,80]{4,3,1,0,2:T(8,128)(2,1)S(1)}, u32[]{:S(2)}, u32[]{:S(2)}) async-start(bf16[1,1,32,72,80]{4,3,1,0,2:T(8,128)(2,1)} %copy.84), calls=%async_computation | async-start | bytes 1179648 | tf_op jit(solution)/shard_map/all_to_all | solution.py:99
  200.1 17.0 %copy-start.9 = (f32[20]{0:T(128)S(1)}, f32[20]{0:T(128)}, u32[]{:S(2)}) copy-start(f32[20]{0:T(128)} %param.25) | copy-start | bytes 244
  207.5 46.1 %all-to-all-start.1 = ((bf16[3,1,16,9,1280]{4,0,3,1,2:T(4,128)(2,1)}), bf16[3,1,16,9,1280]{4,0,3,1,2:T(4,128)(2,1)S(1)}, u32[]{:S(2)}, u32[]{:S(2)}) async-start(bf16[3,1,16,9,1280]{4,0,3,1,2:T(4,128)(2,1)} %bitcast.83), calls=%async_computation.1 | async-start | bytes 2949120 | tf_op jit(solution)/shard_map/all_to_all | solution.py:118
  216.5 95.8 %all-gather.11.cloned.1.call-start = ((), (), s32[]{:S(2)}) async-start(), calls=%async_computation.4 | async-start | bytes 1740800 | tf_op jit(solution)/shard_map/all_gather | solution.py:117
  217.1 117.1 %all-gather.17.cloned.1.call-start = ((), (), s32[]{:S(2)}) async-start(), calls=%async_computation.7 | async-start | bytes 4915200 | tf_op jit(solution)/shard_map/all_gather | solution.py:121
  334.2 9.6 %copy-start.1 = (bf16[3,3,1280,80]{2,3,1,0:T(8,128)(2,1)S(1)}, bf16[3,3,1280,80]{2,3,1,0:T(8,128)(2,1)}, u32[]{:S(2)}) copy-start(bf16[3,3,1280,80]{2,3,1,0:T(8,128)(2,1)} %param.20) | copy-start | bytes 5529604
Sparse Core Ops, SparseCore 0:
  9.2 47.7 all-gather.8
  59.6 102.5 all-gather.12
  164.0 27.7 all-gather.14
  219.6 92.6 all-gather.10
  313.9 20.1 all-gather.16
where the time goes:
time: 357 us; the launch traced here: 351 us
  waiting for transfers between devices  184 us (52%)
  local copies, waits for them, and re-layouts  46 us (13%)
  matrix products  38.8 us (11%)
  blocking collectives  29.6 us (8%)
  other arithmetic  20 us (6%)
  starting transfers between devices  17.1 us (5%)
  between operations  15.1 us (4%)
    all_gather x1, waiting for transfers between devices, local(): whole = lax.all_gather(latent, ROW, axis=2, tiled=True)  49.7 us
    all_gather x1, waiting for transfers between devices, local(): in_half = lax.all_gather(in_half, 'view', axis=0, tiled=False)  48.8 us
    all_to_all x1, waiting for transfers between devices, local(): lax.all_to_all(triple_in, 'view', split_axis=2, concat_axis=1, tiled=True)  36.4 us
    all_to_all x1, blocking collectives, send_back(): lax.all_to_all(mixed, 'view', split_axis=0, concat_axis=1, tiled=True)  29.6 us
    all_gather x1, waiting for transfers between devices, local(): weights_out = lax.all_gather(out_half, 'core', axis=0, tiled=False)  21.1 us
    conv_general_dilated x1, matrix products, local(): lax.conv_general_dilated(activated.reshape(samples * local_views, all_row...  17 us
    all_gather x1, waiting for transfers between devices, local(): out_half = lax.all_gather(out_half, 'view', axis=0, tiled=True)  10.8 us
    all_to_all x1, waiting for transfers between devices, local(): lax.all_to_all(resid_part, ROW, split_axis=2, concat_axis=4, tiled=True)  9.36 us
  transfers between devices with their start and end apart: 7, of which 7 were waited for; matrix products, arithmetic and copies ran while one was open for 22% of the time, Pallas kernels for 0%

commit v1 on v0

--- a/solution.py
+++ b/solution.py
@@ -114,7 +114,9 @@
     ).astype(jnp.bfloat16)
     triple_in = triple_in.reshape((3,) + pixel_major.shape)
     out_half, triple_in = lax.optimization_barrier((out_half, triple_in))
-    out_half = lax.all_gather(out_half, "view", axis=0, tiled=True)
+    out_half = jnp.concatenate(
+        lax.all_to_all(jnp.stack([out_half] * lax.axis_size("view")), "view", 0, 0), axis=0
+    )
     triple_in = lax.all_to_all(triple_in, "view", split_axis=2, concat_axis=1, tiled=True)
     mixed = send_back(attend(triple_in[0], triple_in[1], triple_in[2], head_scale))
     out_half, mixed = lax.optimization_barrier((out_half, mixed))

time: 357 us -> 381 us (1.067)
  blocking collectives: 29.6 us -> 71.6 us
  waiting for transfers between devices: 184 us -> 166 us
    all_to_all x0 -> x1, blocking collectives: none -> 44.1 us  [local(): lax.all_to_all(jnp.stack([out_half] * lax.axis_size('view')), 'view', 0, 0)]
    all_gather x1 -> x0, waiting for transfers between devices: 10.8 us -> none  [local(): out_half = lax.all_gather(out_half, 'view', axis=0, tiled=True)]
    all_gather x1, waiting for transfers between devices: 21.1 us -> 14.8 us  [local(): weights_out = lax.all_gather(out_half, 'core', axis=0, tiled=False)]
    dot_general x1 -> x2, local copies, waits for them, and re-layouts: 0.17 us -> 5.89 us  [local(): jnp.einsum('pc,kcd->pkd', flat_mixed, weights_out, preferred_element_type...]
    all_gather x1 -> x0, local copies, waits for them, and re-layouts: 5.72 us -> none  [local(): weights_out = lax.all_gather(out_half, 'core', axis=0, tiled=False)]
  transfers between devices with their start and end apart: 7 -> 6, of which waited for: 7 -> 6; matrix products, arithmetic and copies ran while one was open for 22% -> 16% of each run, Pallas kernels for 0% -> 0%
where the time goes in v1:
time: 381 us; the launch traced here: 374 us
  waiting for transfers between devices  166 us (44%)
  blocking collectives  71.6 us (19%)
  local copies, waits for them, and re-layouts  45.5 us (12%)
  matrix products  38.8 us (10%)
  other arithmetic  20 us (5%)
  starting transfers between devices  17 us (4%)
  between operations  15.1 us (4%)
    all_gather x1, waiting for transfers between devices, local(): whole = lax.all_gather(latent, ROW, axis=2, tiled=True)  49.7 us
    all_gather x1, waiting for transfers between devices, local(): in_half = lax.all_gather(in_half, 'view', axis=0, tiled=False)  48.8 us
    all_to_all x1, blocking collectives, local(): lax.all_to_all(jnp.stack([out_half] * lax.axis_size('view')), 'view', 0, 0)  44.1 us
    all_to_all x1, waiting for transfers between devices, local(): lax.all_to_all(triple_in, 'view', split_axis=2, concat_axis=1, tiled=True)  35.6 us
    all_to_all x1, blocking collectives, send_back(): lax.all_to_all(mixed, 'view', split_axis=0, concat_axis=1, tiled=True)  27.5 us
    conv_general_dilated x1, matrix products, local(): lax.conv_general_dilated(activated.reshape(samples * local_views, all_row...  17 us
    all_gather x1, waiting for transfers between devices, local(): weights_out = lax.all_gather(out_half, 'core', axis=0, tiled=False)  14.8 us
    all_to_all x1, waiting for transfers between devices, local(): lax.all_to_all(resid_part, ROW, split_axis=2, concat_axis=4, tiled=True)  9.99 us
  transfers between devices with their start and end apart: 6, of which 6 were waited for; matrix products, arithmetic and copies ran while one was open for 16% of the time, Pallas kernels for 0%

profile of v1, /device:TPU:1, one launch (start us, length us, event | category | flops | bytes accessed | tf_op | source)
XLA Modules:
  0.0 374.2 jit_solution(3337870117527379704)
XLA Ops:
  7.3 49.7 %all-gather.8.cloned.1.call-done = bf16[1,1,32,72,1280]{4,3,1,0,2:T(8,128)(2,1)} async-done(((bf16[1,1,2,72,1280]{4,3,1,0,2:T(8,128)(2,1)}), bf16[1,1,32,72,1280]{4,3,1,0,2:T(8,128)(2,1)}) %all-gather.8.cloned.1.call-update) | async-done | bytes 5898256 | tf_op jit(solution)/shard_map/all_gather | solution.py:55
  61.2 3.4 convolution_reduce_fusion
  67.9 6.8 %copy.78 = bf16[1,1,32,72,1280]{4,2,3,1,0:T(8,128)(2,1)} copy(bf16[1,1,32,72,1280]{4,3,1,0,2:T(8,128)(2,1)} %all-gather.8.cloned.1.call-done) | data formatting | bytes 11796480 | tf_op jit(solution)/shard_map/optimization_barrier | solution.py:56
  75.9 4.5 %fusion.4 = f32[1280]{0:T(1024)S(1)} fusion(f32[1280]{0:T(1024)S(1)} %sub.48, bf16[1,1,32,72,1280]{4,3,1,0,2:T(8,128)(2,1)} %all-gather.8.cloned.1.call-done), kind=kLoop, calls=%fused_computation.7 | loop fusion | flops 11795200 | bytes 5908480 | tf_op jit(solution)/shard_map/reduce_sum | solution.py:70
  80.8 8.7 %fusion.16 = bf16[32,1,72,1280]{3,0,2,1:T(8,128)(2,1)S(1)} fusion(f32[1280]{0:T(1024)S(1)} %copy-done.4, f32[1280]{0:T(1024)S(1)} %copy-done.3, f32[1280]{0:T(1024)S(1)} %copy-done.6, f32[1280]{0:T(1024)S(1)} %copy-done.7, f32[1280]{0:T(1024)S(1)} %mul.96, f32[1280]{0:T(1024)S(1)} %sub.48, bf16[1,1,32,72,1280]{4,3,1,0,2:T(8,128)(2,1)} %all-gather.8.cloned.1.call-done), kind=kLoop, calls=%fused_computation.19 | loop fusion | flops 35389440 | bytes 11827200 | tf_op jit(solution)/shard_map/reshape | solution.py:86
  90.3 3.6 copy.81
  94.3 17.0 %fusion.23 = f32[32,8,10,80]{3,1,2,0:T(8,128)S(1)} fusion(bf16[3,3,1280,80]{2,3,1,0:T(8,128)(2,1)S(1)} %copy-done, bf16[32,1,7,2,1280]{4,2,3,0,1:T(8,128)(2,1)S(1)} %slice.28, bf16[32,1,8,10,1280]{4,2,3,0,1:T(8,128)(2,1)S(1)} %copy.81, pred[8,10]{0,1:T(8,128)(4,1)S(1)} %copy-done.10), kind=kOutput, calls=%fused_computation.31 | convolution fusion | flops 4644085760 | bytes 10362960 | tf_op jit(solution)/shard_map/conv_general_dilated | solution.py:85
  113.4 48.8 %all-gather.10.cloned.1.call-done = bf16[48,640,80]{1,2,0:T(8,128)(2,1)} async-done(((bf16[3,640,80]{1,2,0:T(8,128)(2,1)}), bf16[48,640,80]{1,2,0:T(8,128)(2,1)}) %all-gather.10.cloned.1.call-update) | async-done | bytes 4915216 | tf_op jit(solution)/shard_map/all_gather | solution.py:61
  163.2 7.9 %all-to-all-start = ((bf16[1,1,32,72,80]{4,3,1,0,2:T(8,128)(2,1)}), bf16[1,1,32,72,80]{4,3,1,0,2:T(8,128)(2,1)S(1)}, u32[]{:S(2)}, u32[]{:S(2)}) async-start(bf16[1,1,32,72,80]{4,3,1,0,2:T(8,128)(2,1)} %copy.83), calls=%async_computation | async-start | bytes 1179648 | tf_op jit(solution)/shard_map/all_to_all | solution.py:99
  171.2 10.0 %all-to-all-done = bf16[1,1,32,72,80]{4,3,1,0,2:T(8,128)(2,1)S(1)} async-done(((bf16[1,1,32,72,80]{4,3,1,0,2:T(8,128)(2,1)}), bf16[1,1,32,72,80]{4,3,1,0,2:T(8,128)(2,1)S(1)}, u32[]{:S(2)}, u32[]{:S(2)}) %all-to-all-start) | async-done | bytes 368672 | tf_op jit(solution)/shard_map/all_to_all | solution.py:99
  185.3 6.5 %all-gather.12.cloned.1.call-done = bf16[32,3,640,80]{2,3,1,0:T(8,128)(2,1)} async-done(((bf16[16,3,640,80]{2,3,1,0:T(8,128)(2,1)}), bf16[32,3,640,80]{2,3,1,0:T(8,128)(2,1)}) %all-gather.12.cloned.1.call-update) | async-done | bytes 9830416 | tf_op jit(solution)/shard_map/all_gather | solution.py:98
  191.8 8.2 %fusion.38 = bf16[16,3,80,144,1]{2,3,1,0,4:T(8,128)(2,1)S(1)} fusion(bf16[2,16,3,640,80]{3,4,2,1,0:T(8,128)(2,1)} %bitcast.93, f32[144,2,640]{2,1,0:T(2,128)S(1)} %reshape.205, f32[2,640]{1,0:T(2,128)S(1)} %mul.106, f32[144]{0:T(256)S(1)} %rsqrt.21, f32[144]{0:T(256)S(1)} %div.35), kind=kOutput, calls=%fused_computation.53 | convolution fusion | flops 1416314880 | bytes 11679872 | tf_op jit(solution)/shard_map/pkc,kjmcd->mpjd/dot_general | solution.py:112
  201.8 5.7 %reshape.194 = bf16[3,1,16,9,1280]{4,0,3,2,1:T(4,128)(2,1)} reshape(bf16[3,144,16,80]{3,2,0,1:T(8,128)(2,1)} %copy.87) | data formatting | bytes 2211840 | tf_op jit(solution)/shard_map/reshape | solution.py:115
  207.5 9.0 %all-to-all-start.2 = ((bf16[3,1,16,9,1280]{4,0,3,1,2:T(4,128)(2,1)}), bf16[3,1,16,9,1280]{4,0,3,1,2:T(4,128)(2,1)S(1)}, u32[]{:S(2)}, u32[]{:S(2)}) async-start(bf16[3,1,16,9,1280]{4,0,3,1,2:T(4,128)(2,1)} %bitcast.85), calls=%async_computation.2 | async-start | bytes 2949120 | tf_op jit(solution)/shard_map/all_to_all | solution.py:120
  216.6 35.6 %all-to-all-done.2 = bf16[3,1,16,9,1280]{4,0,3,1,2:T(4,128)(2,1)S(1)} async-done(((bf16[3,1,16,9,1280]{4,0,3,1,2:T(4,128)(2,1)}), bf16[3,1,16,9,1280]{4,0,3,1,2:T(4,128)(2,1)S(1)}, u32[]{:S(2)}, u32[]{:S(2)}) %all-to-all-start.2) | async-done | bytes 1105952 | tf_op jit(solution)/shard_map/all_to_all | solution.py:120
  252.2 6.4 %slice_reduce_fusion.2 = (bf16[16,9,1280]{2,1,0:T(8,128)(2,1)S(1)}, bf16[16,9,1280]{2,1,0:T(8,128)(2,1)}, bf16[16,9,1280]{2,1,0:T(8,128)(2,1)}) fusion(bf16[3,1,16,9,1280]{4,0,3,1,2:T(4,128)(2,1)S(1)} %all-to-all-done.2), kind=kLoop, calls=%fused_computation.43 | loop fusion | bytes 2211840 | tf_op jit(solution)/shard_map/slice | solution.py:121
  260.3 2.5 reshape.228
  264.4 3.2 fusion.56
  267.5 2.1 fusion.26
  270.5 27.5 %all_to_all.35 = bf16[16,1,9,1280]{3,2,1,0:T(8,128)(2,1)S(1)} all-to-all(bf16[16,1,9,1280]{3,2,1,0:T(8,128)(2,1)S(1)} %reshape.229), channel_id=1, replica_groups=mesh['view'=16,'chip'=8,'core'=2] {'view'}, dimensions={0} | all-to-all | bytes 737280 | tf_op jit(solution)/shard_map/all_to_all | solution.py:34
  298.1 44.1 %all_to_all.36 = bf16[16,80,640]{2,1,0:T(8,128)(2,1)} all-to-all(bf16[16,80,640]{2,1,0:T(8,128)(2,1)S(1)} %stack.2), channel_id=1, replica_groups=mesh['view'=16,'chip'=8,'core'=2] {'view'}, dimensions={0} | all-to-all | bytes 3276800 | tf_op jit(solution)/shard_map/all_to_all | solution.py:118
  342.9 14.8 %all-gather.14.cloned.1.call-done = bf16[2560,640]{1,0:T(8,128)(2,1)} async-done(((bf16[1280,640]{1,0:T(8,128)(2,1)}), bf16[2560,640]{1,0:T(8,128)(2,1)}) %all-gather.14.cloned.1.call-update) | async-done | bytes 3276816 | tf_op jit(solution)/shard_map/all_gather | solution.py:123
  357.8 5.7 %copy.98 = bf16[2,640,1280]{2,1,0:T(8,128)(2,1)} copy(bf16[2,640,1280]{1,2,0:T(8,128)(2,1)} %bitcast.90) | data formatting | bytes 6553600 | tf_op jit(solution)/shard_map/pc,kcd->pkd/dot_general | solution.py:128
  363.5 3.9 %fusion.19 = bf16[1,1,2,72,1280]{4,3,2,1,0:T(8,128)(2,1)} fusion(f32[2,72,1280]{2,1,0:T(8,128)S(1)} %reshape.204, bf16[2,72,1280]{2,1,0:T(8,128)(2,1)S(1)} %dot_general.29, bf16[1280,1280,1]{1,0,2:T(8,128)(2,1)} %bitcast.80), kind=kOutput, calls=%fused_computation.24 | convolution fusion | flops 472227840 | bytes 4751360 | tf_op jit(solution)/shard_map/pc,kcd->pkd/dot_general | solution.py:128
  (80 shorter events, 23.7 us)
Async XLA Ops:
  6.5 87.7 %copy-start = (bf16[3,3,1280,80]{2,3,1,0:T(8,128)(2,1)S(1)}, bf16[3,3,1280,80]{2,3,1,0:T(8,128)(2,1)}, u32[]{:S(2)}) copy-start(bf16[3,3,1280,80]{2,3,1,0:T(8,128)(2,1)} %param.20) | copy-start | bytes 5529604
  6.5 50.4 %all-gather.8.cloned.1.call-start = ((), (), s32[]{:S(2)}) async-start(), calls=%async_computation.4 | async-start | bytes 6266880 | tf_op jit(solution)/shard_map/all_gather | solution.py:55
  7.3 154.9 %all-gather.10.cloned.1.call-start = ((), (), s32[]{:S(2)}) async-start(), calls=%async_computation.5 | async-start | bytes 5222400 | tf_op jit(solution)/shard_map/all_gather | solution.py:61
  58.7 133.1 %all-gather.12.cloned.1.call-start = ((), (), s32[]{:S(2)}) async-start(), calls=%async_computation.6 | async-start | bytes 14745600 | tf_op jit(solution)/shard_map/all_gather | solution.py:98
  61.2 13.4 %slice-start = ((s8[5898240]{0:T(1024)(128)(4,1)}), s8[1703936]{0:T(1024)(128)(4,1)S(1)}, s32[]{:S(2)}) async-start(s8[5898240]{0:T(1024)(128)(4,1)} %bitcast.77), calls=%async_computation.8 | async-start | bytes 3407872
  67.9 6.8 %slice-start.1 = ((s8[5898240]{0:T(1024)(128)(4,1)}), s8[4194304]{0:T(1024)(128)(4,1)S(1)}, s32[]{:S(2)}) async-start(s8[5898240]{0:T(1024)(128)(4,1)} %bitcast.77), calls=%async_computation.9 | async-start | bytes 8388608
  75.5 5.3 %copy-start.3 = (f32[1280]{0:T(1024)S(1)}, f32[1280]{0:T(1024)}, u32[]{:S(2)}) copy-start(f32[1280]{0:T(1024)} %get-tuple-element.26) | copy-start | bytes 15364
  75.5 5.3 %copy-start.4 = (f32[1280]{0:T(1024)S(1)}, f32[1280]{0:T(1024)}, u32[]{:S(2)}) copy-start(f32[1280]{0:T(1024)} %get-tuple-element.27) | copy-start | bytes 15364
  75.5 5.3 %copy-start.6 = (f32[1280]{0:T(1024)S(1)}, f32[1280]{0:T(1024)}, u32[]{:S(2)}) copy-start(f32[1280]{0:T(1024)} %param.15) | copy-start | bytes 15364
  75.5 5.3 %copy-start.7 = (f32[1280]{0:T(1024)S(1)}, f32[1280]{0:T(1024)}, u32[]{:S(2)}) copy-start(f32[1280]{0:T(1024)} %param.14) | copy-start | bytes 15364
  90.3 4.0 %copy-start.10 = (pred[8,10]{0,1:T(8,128)(4,1)S(1)}, pred[8,10]{0,1:T(8,128)(4,1)}, u32[]{:S(2)}) copy-start(pred[8,10]{0,1:T(8,128)(4,1)} %constant.46) | copy-start | bytes 244
  94.3 17.4 %copy-start.8 = (f32[80]{0:T(128)S(1)}, f32[80]{0:T(128)}, u32[]{:S(2)}) copy-start(f32[80]{0:T(128)} %dynamic_slice.14) | copy-start | bytes 964
  111.7 59.4 %copy-start.5 = (f32[1280]{0:T(1024)S(1)}, f32[1280]{0:T(1024)}, u32[]{:S(2)}) copy-start(f32[1280]{0:T(1024)} %param.22) | copy-start | bytes 15364
  111.7 59.5 %copy-start.2 = (bf16[80,1280]{1,0:T(8,128)(2,1)S(1)}, bf16[80,1280]{1,0:T(8,128)(2,1)}, u32[]{:S(2)}) copy-start(bf16[80,1280]{1,0:T(8,128)(2,1)} %param.24) | copy-start | bytes 614404
  163.2 17.9 %all-to-all-start = ((bf16[1,1,32,72,80]{4,3,1,0,2:T(8,128)(2,1)}), bf16[1,1,32,72,80]{4,3,1,0,2:T(8,128)(2,1)S(1)}, u32[]{:S(2)}, u32[]{:S(2)}) async-start(bf16[1,1,32,72,80]{4,3,1,0,2:T(8,128)(2,1)} %copy.83), calls=%async_computation | async-start | bytes 1179648 | tf_op jit(solution)/shard_map/all_to_all | solution.py:99
  200.1 16.4 %copy-start.9 = (f32[20]{0:T(128)S(1)}, f32[20]{0:T(128)}, u32[]{:S(2)}) copy-start(f32[20]{0:T(128)} %param.25) | copy-start | bytes 244
  207.5 44.7 %all-to-all-start.2 = ((bf16[3,1,16,9,1280]{4,0,3,1,2:T(4,128)(2,1)}), bf16[3,1,16,9,1280]{4,0,3,1,2:T(4,128)(2,1)S(1)}, u32[]{:S(2)}, u32[]{:S(2)}) async-start(bf16[3,1,16,9,1280]{4,0,3,1,2:T(4,128)(2,1)} %bitcast.85), calls=%async_computation.2 | async-start | bytes 2949120 | tf_op jit(solution)/shard_map/all_to_all | solution.py:120
  216.5 141.3 %all-gather.14.cloned.1.call-start = ((), (), s32[]{:S(2)}) async-start(), calls=%async_computation.7 | async-start | bytes 4915200 | tf_op jit(solution)/shard_map/all_gather | solution.py:123
  357.8 9.6 %copy-start.1 = (bf16[3,3,1280,80]{2,3,1,0:T(8,128)(2,1)S(1)}, bf16[3,3,1280,80]{2,3,1,0:T(8,128)(2,1)}, u32[]{:S(2)}) copy-start(bf16[3,3,1280,80]{2,3,1,0:T(8,128)(2,1)} %param.20) | copy-start | bytes 5529604
Sparse Core Ops, SparseCore 0:
  9.2 47.7 all-gather.7
  59.6 102.5 all-gather.9
  164.0 27.7 all-gather.11
  342.4 15.3 all-gather.13
